TPU v7x, 128 devices: a whole 4x4x4 slice. The times are simulated.
128 devices in a mesh: req: 32 (over x, z, core), tensor: 4 (over y).
Axes of the slice: x: 4, y: 4, z: 4, core: 2. Of those that a mesh axis runs over, the one named last changes fastest.
Arguments:
- hidden_in: bfloat16 [32768, 2048], P('req', 'tensor'), may hold values from -6 to 6
- segment: int32 [32768], P('req'), may hold values from 0 to 15, never falling along the last dimension, each value on 1 to 4096 neighbouring positions
- w_query: bfloat16 [2048, 1024], P(None, 'tensor'), may hold values from -0.125 to 0.125
- w_key: bfloat16 [2048, 1024], P(None, 'tensor'), may hold values from -0.125 to 0.125
- w_value: bfloat16 [2048, 2048], P(None, 'tensor'), may hold values from -0.125 to 0.125
- w_outgate: bfloat16 [2048, 2048], P(None, 'tensor'), may hold values from -0.125 to 0.125
- w_gate_down: bfloat16 [2048, 16], replicated, may hold values from -0.125 to 0.125
- w_gate_up: bfloat16 [16, 1024], P(None, 'tensor'), may hold values from -1.5 to 1.5
- gate_bias: float32 [1024], P('tensor'), may hold values from -2 to 8
- norm_gain: float32 [512], replicated, may hold values from 0.5 to 1.5
- w_out: bfloat16 [2048, 2048], P('tensor'), may hold values from -0.125 to 0.125
Outputs:
- mixed: bfloat16 [32768, 2048], P('req', 'tensor')
Inputs may be any that keep to these rules, and one draw needn't show every extreme that they name: segment never falls along the tokens; each prompt covers 1 to 4096 consecutive tokens and one covers exactly 4096.
All inputs are finite; a program needn't handle non-finite values.
Results may differ from a plain program's by a relative error of at most 0.014.
Values may be sent and summed in bfloat16 or wider, within the bound.
No kernel may reach another device: no remote copies, remote signals or barrier semaphores. Data moves between devices by JAX's collectives and lax.ppermute only.
A program may use at most 128 MiB of HBM per device.

v0:
```python
import jax
import jax.numpy as jnp
from jax import lax
from jax.sharding import PartitionSpec as P

GROUP = 64
PIECES = 4
SEG_MOST = 4096
HIGHEST = lax.Precision.HIGHEST


def shifted(x, axis, shift, devices):
    pairs = [(i, i + shift) for i in range(devices - shift)]
    return lax.ppermute(x, axis, pairs)


def body(
    hidden_in,
    segment,
    w_query,
    w_key,
    w_value,
    w_outgate,
    w_gate_down,
    w_gate_up,
    gate_bias,
    norm_gain,
    w_out,
):
    tok_rows = hidden_in.shape[0]
    key_width = w_query.shape[1]
    value_width = w_value.shape[1]
    weights = (w_query, w_key, w_value, w_outgate, w_gate_down)
    piece_rows = tok_rows // PIECES
    piece_blocks = piece_rows // GROUP
    blocks = tok_rows // GROUP
    positions = jnp.arange(GROUP)
    causal = positions[None, :] <= positions[:, None]
    starts = jnp.concatenate(
        [jnp.zeros((1,), jnp.int32), (segment[1:] != segment[:-1]).astype(jnp.int32)]
    )
    live_device = (jnp.cumsum(starts) == 0).astype(jnp.float32)
    seg_all = segment.reshape(blocks, GROUP)
    live_all = (jnp.cumsum(starts.reshape(blocks, GROUP), axis=1) == 0).astype(jnp.float32)
    parts = []
    for p in range(PIECES):
        rows = slice(p * piece_rows, (p + 1) * piece_rows)
        piece = lax.all_gather(hidden_in[rows], "tensor", axis=1, tiled=True)
        query_sum, key_sum, value_sum, outgate, low = tuple(
            (jnp.dot(piece, weight, preferred_element_type=jnp.float32) for weight in weights)
        )
        query = query_sum.astype(jnp.bfloat16)
        key = key_sum.astype(jnp.bfloat16)
        value = value_sum.astype(jnp.bfloat16)
        pre_gate = jnp.dot(low, w_gate_up.astype(jnp.float32), precision=HIGHEST) + gate_bias
        logdecay = jax.nn.log_sigmoid(pre_gate) / 16.0
        chunks = slice(p * piece_blocks, (p + 1) * piece_blocks)
        seg_blocks = seg_all[chunks]
        live_blocks = live_all[chunks]
        cumul = jnp.cumsum(logdecay.reshape(piece_blocks, GROUP, key_width), axis=1)
        q_float = query.astype(jnp.float32).reshape(piece_blocks, GROUP, key_width)
        k_float = key.astype(jnp.float32).reshape(piece_blocks, GROUP, key_width)
        v_float = value.astype(jnp.float32).reshape(piece_blocks, GROUP, value_width)
        centre = cumul[:, GROUP // 2, :]
        q_scaled = q_float * jnp.exp(cumul - centre[:, None, :])
        k_scaled = k_float * jnp.exp(centre[:, None, :] - cumul)
        raw_scores = jnp.einsum("ncd,nsd->ncs", q_scaled, k_scaled, precision=HIGHEST)
        allowed = causal[None] & (seg_blocks[:, :, None] == seg_blocks[:, None, :])
        scores = jnp.where(allowed, raw_scores, 0.0)
        intra = jnp.einsum("ncs,nsv->ncv", scores, v_float, precision=HIGHEST)
        block_totals = cumul[:, -1, :]
        same_last = (seg_blocks == seg_blocks[:, -1:]).astype(jnp.float32)
        k_decayed = k_float * jnp.exp(block_totals[:, None, :] - cumul) * same_last[:, :, None]
        chunk_states = jnp.einsum("ncd,ncv->ndv", k_decayed, v_float, precision=HIGHEST)
        chunk_decay = jnp.exp(block_totals) * live_blocks[:, -1:]
        parts.append(
            (
                query,
                outgate,
                q_float,
                cumul,
                live_blocks,
                intra,
                chunk_states,
                chunk_decay,
                block_totals,
            )
        )
    entering = jnp.zeros((key_width, value_width), jnp.float32)
    local_outs = []
    for p in range(PIECES):
        query, outgate, q_float, cumul, live_blocks, intra, chunk_states, chunk_decay, _ = parts[p]
        states = []
        for n in range(piece_blocks):
            states.append(entering)
            entering = chunk_decay[n][:, None] * entering + chunk_states[n]
        inter = (
            jnp.einsum(
                "ncd,ndv->ncv", q_float * jnp.exp(cumul), jnp.stack(states), precision=HIGHEST
            )
            * live_blocks[:, :, None]
        )
        local_outs.append((intra + inter).reshape(piece_rows, value_width))
    final_state = entering
    block_totals = jnp.concatenate([part[8] for part in parts])
    before = jnp.cumsum(block_totals, axis=0) - block_totals
    cumul = jnp.concatenate([part[3] for part in parts])
    device_cumul = (cumul + before[:, None, :]).reshape(tok_rows, key_width)
    devices = lax.axis_size("req")
    window = min(devices - 1, -(-SEG_MOST // tok_rows))
    first_id = (segment[0] + 1).astype(jnp.float32)
    last_id = (segment[-1] + 1).astype(jnp.float32)
    decay_device = jnp.exp(device_cumul[-1]) * live_device[-1]
    tail = jnp.zeros((2, value_width), jnp.float32)
    tail = tail.at[0, :key_width].set(decay_device).at[1, 0].set(first_id).at[1, 1].set(last_id)
    message = jnp.concatenate([final_state, tail]).astype(jnp.bfloat16)
    got = [shifted(message, "req", j, devices).astype(jnp.float32) for j in range(1, window + 1)]
    state_in = got[-1][:key_width]
    last_far = got[-1][key_width + 1, 1]
    for j in range(window - 1, 0, -1):
        msg = got[j - 1]
        link = (msg[key_width + 1, 0] == last_far).astype(jnp.float32)
        state_in = msg[:key_width] + (link * msg[key_width, :key_width])[:, None] * state_in
        last_far = msg[key_width + 1, 1]
    linked = (first_id == last_far).astype(jnp.float32)
    mask = live_device * linked
    outs = []
    for p in range(PIECES):
        rows = slice(p * piece_rows, (p + 1) * piece_rows)
        query, outgate = (parts[p][0], parts[p][1])
        carried = jnp.dot(
            query.astype(jnp.float32) * jnp.exp(device_cumul[rows]), state_in, precision=HIGHEST
        )
        attn = (local_outs[p] + carried * mask[rows][:, None]) * key_width ** (-0.5)
        normed = attn * lax.rsqrt(jnp.mean(attn * attn, axis=-1, keepdims=True) + 1e-05) * norm_gain
        gated = (normed * jax.nn.silu(outgate)).astype(jnp.bfloat16)
        head_term = jnp.dot(gated, w_out, preferred_element_type=jnp.float32)
        outs.append(
            lax.psum_scatter(
                head_term.astype(jnp.bfloat16), "tensor", scatter_dimension=1, tiled=True
            )
        )
    return jnp.concatenate(outs, axis=0)


def solution(mesh):
    in_specs = (
        P("req", "tensor"),
        P("req"),
        P(None, "tensor"),
        P(None, "tensor"),
        P(None, "tensor"),
        P(None, "tensor"),
        P(),
        P(None, "tensor"),
        P("tensor"),
        P(),
        P("tensor", None),
    )
    out_specs = P("req", "tensor")
    return jax.shard_map(body, mesh=mesh, in_specs=in_specs, out_specs=out_specs, check_vma=False)
```

profile of v0, /device:TPU:0, one launch (start us, length us, event | category | flops | bytes accessed | tf_op | source)
XLA Modules:
  0.0 292.2 jit_solution(15862725786038252527)
XLA Ops:
  6.6 2.3 fusion.172
  9.0 0.7 all-gather.7.cloned.1.call-update
  9.7 0.7 all-gather.11.cloned.1.call-update
  11.1 0.6 fusion.182
  17.1 0.7 compare_convert_fusion.1
  18.4 0.7 slice.495
  19.7 16.0 %all-gather.5.cloned.1.call-done = bf16[256,2048]{1,0:T(8,128)(2,1)} async-done(((bf16[256,512]{1,0:T(8,128)(2,1)}), bf16[256,2048]{1,0:T(8,128)(2,1)}) %all-gather.5.cloned.1.call-update) | async-done | bytes 1048592 | tf_op jit(solution)/shard_map/all_gather | solution.py:48
  35.7 1.6 fusion.194
  38.0 0.6 fusion.176
  38.7 23.2 %all-gather.7.cloned.1.call-done = bf16[256,2048]{1,0:T(8,128)(2,1)} async-done(((bf16[256,512]{1,0:T(8,128)(2,1)}), bf16[256,2048]{1,0:T(8,128)(2,1)}) %all-gather.7.cloned.1.call-update) | async-done | bytes 1048592 | tf_op jit(solution)/shard_map/all_gather | solution.py:48
  61.8 1.6 fusion.196
  64.7 23.2 %all-gather.11.cloned.1.call-done = bf16[256,2048]{1,0:T(8,128)(2,1)} async-done(((bf16[256,512]{1,0:T(8,128)(2,1)}), bf16[256,2048]{1,0:T(8,128)(2,1)}) %all-gather.11.cloned.1.call-update) | async-done | bytes 1048592 | tf_op jit(solution)/shard_map/all_gather | solution.py:48
  88.0 1.6 fusion.198
  92.2 21.8 %all-gather.9.cloned.1.call-done = bf16[256,2048]{1,0:T(8,128)(2,1)} async-done(((bf16[256,512]{1,0:T(8,128)(2,1)}), bf16[256,2048]{1,0:T(8,128)(2,1)}) %all-gather.9.cloned.1.call-update) | async-done | bytes 1048592 | tf_op jit(solution)/shard_map/all_gather | solution.py:48
  114.0 1.6 fusion.197
  116.3 0.6 fusion.178
  117.0 0.6 fusion.184
  118.4 1.1 slice_exponential_fusion.3
  120.9 0.7 convolution_convert_fusion.7
  121.7 1.2 fusion.82
  123.5 0.7 convolution_convert_fusion.5
  124.3 1.2 fusion.88
  126.0 0.7 convolution_convert_fusion.4
  126.8 1.2 fusion.91
  128.6 0.7 convolution_convert_fusion.6
  129.5 1.2 fusion.85
  130.8 3.8 %multiply_add_fusion = (f32[1,256,512]{2,1,0:T(8,128)}, f32[1,256,512]{2,1,0:T(8,128)}, f32[1,256,512]{2,1,0:T(8,128)}, f32[1,256,512]{2,1,0:T(8,128)}, f32[1,25...) fusion(f32[4,256,512]{2,1,0:T(8,128)S(1)} %fusion.91, ...), kind=kLoop, calls=%fused_computation.127 | loop fusion | flops 3801088 | bytes 15744000 | tf_op jit(solution)/shard_map/add | solution.py:96
  134.7 1.5 fusion.65
  136.2 1.2 scatter.11
  137.4 1.3 scatter.14
  138.6 1.0 pad_maximum_fusion.1
  139.7 5.2 %collective-permute-start.3 = (bf16[258,512]{1,0:T(8,128)(2,1)S(1)}, bf16[258,512]{1,0:T(8,128)(2,1)S(1)}, u32[]{:S(2)}, u32[]{:S(2)}) collective-permute-start(bf16[258,512]{1,0:T(8,128)(2,1)S(1)} %pad_maximum_fusion.1), channel_id=1, source_target_pairs={{0,16},{4,20},{8,24},{12,28},{16,32},{20,36},{24,40},{28,44},{32,4... | collective-permute-start | bytes 792584 | tf_op jit(solution)/shard_map/ppermute | solution.py:14
  144.9 1.3 collective-permute-start.2
  146.2 2.6 collective-permute-start.1
  148.8 4.5 %collective-permute-start = (bf16[258,512]{1,0:T(8,128)(2,1)S(1)}, bf16[258,512]{1,0:T(8,128)(2,1)S(1)}, u32[]{:S(2)}, u32[]{:S(2)}) collective-permute-start(bf16[258,512]{1,0:T(8,128)(2,1)S(1)} %pad_maximum_fusion.1), channel_id=1, source_target_pairs={{0,4},{4,8},{8,12},{12,16},{16,20},{20,24},{24,28},{28,32},{32,36}... | collective-permute-start | bytes 792584 | tf_op jit(solution)/shard_map/ppermute | solution.py:14
  153.4 2.4 bitcast_multiply_fusion
  156.3 1.4 fusion.31
  157.7 1.1 convolution_add_fusion
  158.9 0.7 slice.584
  159.6 0.7 copy-done.50
  162.2 0.7 copy-done.51
  164.9 0.7 copy-done.52
  168.7 1.0 convert_element_type.190
  169.8 1.0 convert_element_type.187
  170.8 1.1 convert_element_type.186
  172.2 0.8 copy-done.3
  173.0 1.5 multiply_reduce_fusion
  175.0 4.4 %convolution_convert_fusion = bf16[256,2048]{1,0:T(8,128)(2,1)} fusion(bf16[512,2048]{1,0:T(8,128)(2,1)S(1)} %copy-done, f32[256,512]{1,0:T(8,128)} %get-tuple-element.117, f32[256]{0:T(256)} %rsqrt_multiply_fusion, f32[512]{0:T(512)} %param.26, bf16[256,2048]{1,0:T(8,128)(2,1)} %all-gather.11.cloned.1.call-done, bf16[2048,512]{1,0:T(8,128)(2,1)} %param.22), kind=kOutput, calls=%fused_computation | convolution fusion | flops 1075314688 | bytes 6818816 | tf_op jit(solution)/shard_map/dot_general | solution.py:137
  179.5 1.9 bitcast_multiply_fusion.1
  181.5 2.1 fusion.34
  184.7 1.5 multiply_reduce_fusion.1
  186.7 4.4 %convolution_convert_fusion.1 = bf16[256,2048]{1,0:T(8,128)(2,1)} fusion(bf16[512,2048]{1,0:T(8,128)(2,1)S(1)} %copy-done, f32[256,512]{1,0:T(8,128)} %get-tuple-element.121, f32[256]{0:T(256)} %rsqrt_multiply_fusion.1, f32[512]{0:T(512)} %param.26, bf16[256,2048]{1,0:T(8,128)(2,1)} %all-gather.9.cloned.1.call-done, bf16[2048,512]{1,0:T(8,128)(2,1)} %param.22), kind=kOutput, calls=%fused_computation.1 | convolution fusion | flops 1075314688 | bytes 6818816 | tf_op jit(solution)/shard_map/dot_general | solution.py:137
  191.5 1.8 bitcast_multiply_fusion.2
  193.4 2.1 fusion.37
  196.6 1.5 multiply_reduce_fusion.2
  198.1 4.4 %convolution_convert_fusion.2 = bf16[256,2048]{1,0:T(8,128)(2,1)} fusion(bf16[512,2048]{1,0:T(8,128)(2,1)S(1)} %copy-done, f32[256,512]{1,0:T(8,128)} %get-tuple-element.125, f32[256]{0:T(256)S(1)} %rsqrt_multiply_fusion.2, f32[512]{0:T(512)S(1)} %copy-done.102, bf16[256,2048]{1,0:T(8,128)(2,1)} %all-gather.7.cloned.1.call-done, bf16[2048,512]{1,0:T(8,128)(2,1)} %param.22), kind=kOutput, calls=%fused_computation.2 | convolution fusion | flops 1075314688 | bytes 6818816 | tf_op jit(solution)/shard_map/dot_general | solution.py:137
  202.6 1.8 bitcast_multiply_fusion.3
  205.4 1.4 fusion.43
  206.8 1.5 multiply_reduce_fusion.3
  208.3 4.1 %convolution_convert_fusion.3 = bf16[256,2048]{1,0:T(8,128)(2,1)} fusion(bf16[512,2048]{1,0:T(8,128)(2,1)S(1)} %copy-done, f32[256,512]{1,0:T(8,128)} %get-tuple-element.129, f32[512]{0:T(512)S(1)} %copy-done.103, f32[256]{0:T(256)S(1)} %rsqrt_multiply_fusion.3, bf16[256,2048]{1,0:T(8,128)(2,1)S(1)} %copy-done.8, bf16[2048,512]{1,0:T(8,128)(2,1)} %param.22), kind=kOutput, calls=%fused_computation.3 | convolution fusion | flops 1075314688 | bytes 6818816 | tf_op jit(solution)/shard_map/dot_general | solution.py:137
  212.4 18.9 %reduce-scatter.9.cloned.1.call-done = bf16[256,512]{1,0:T(8,128)(2,1)} async-done(((bf16[256,2048]{1,0:T(8,128)(2,1)}), bf16[256,512]{1,0:T(8,128)(2,1)}) %reduce-scatter.9.cloned.1.call-update) | async-done | bytes 262160 | tf_op jit(solution)/shard_map/reduce_scatter | solution.py:139
  231.3 25.9 %reduce-scatter.7.cloned.1.call-done = bf16[256,512]{1,0:T(8,128)(2,1)} async-done(((bf16[256,2048]{1,0:T(8,128)(2,1)}), bf16[256,512]{1,0:T(8,128)(2,1)}) %reduce-scatter.7.cloned.1.call-update) | async-done | bytes 262160 | tf_op jit(solution)/shard_map/reduce_scatter | solution.py:139
  257.2 25.9 %reduce-scatter.5.cloned.1.call-done = bf16[256,512]{1,0:T(8,128)(2,1)} async-done(((bf16[256,2048]{1,0:T(8,128)(2,1)}), bf16[256,512]{1,0:T(8,128)(2,1)}) %reduce-scatter.5.cloned.1.call-update) | async-done | bytes 262160 | tf_op jit(solution)/shard_map/reduce_scatter | solution.py:139
  283.1 2.2 pad_maximum_fusion
  (305 shorter events, 22.7 us)
Async XLA Ops:
  6.5 168.5 %copy-start = (bf16[512,2048]{1,0:T(8,128)(2,1)S(1)}, bf16[512,2048]{1,0:T(8,128)(2,1)}, u32[]{:S(2)}) copy-start(bf16[512,2048]{1,0:T(8,128)(2,1)} %param.27) | copy-start | bytes 6291460
  6.5 4.5 %copy-start.69 = (s32[1024]{0:T(1024)S(1)}, s32[1024]{0:T(1024)}, u32[]{:S(2)}) copy-start(s32[1024]{0:T(1024)} %param.18) | copy-start | bytes 12292
  6.5 29.2 %copy-start.27 = (bf16[2048,16]{0,1:T(8,128)(2,1)S(1)}, bf16[2048,16]{0,1:T(8,128)(2,1)}, u32[]{:S(2)}) copy-start(bf16[2048,16]{0,1:T(8,128)(2,1)} %param.23) | copy-start | bytes 196612
  6.5 30.8 %copy-start.104 = (f32[256]{0:T(256)S(1)}, f32[256]{0:T(256)}, u32[]{:S(2)}) copy-start(f32[256]{0:T(256)} %param.25) | copy-start | bytes 3076
  6.5 30.8 %copy-start.101 = (bf16[16,256]{1,0:T(8,128)(2,1)S(1)}, bf16[16,256]{1,0:T(8,128)(2,1)}, u32[]{:S(2)}) copy-start(bf16[16,256]{1,0:T(8,128)(2,1)} %param.24) | copy-start | bytes 24580
  6.5 29.1 %all-gather.5.cloned.1.call-start = ((), (), s32[]{:S(2)}) async-start(), calls=%async_computation.4 | async-start | bytes 1310720 | tf_op jit(solution)/shard_map/all_gather | solution.py:48
  8.9 52.9 %all-gather.7.cloned.1.call-start = ((), (), s32[]{:S(2)}) async-start(), calls=%async_computation.5 | async-start | bytes 1310720 | tf_op jit(solution)/shard_map/all_gather | solution.py:48
  9.7 78.3 %all-gather.11.cloned.1.call-start = ((), (), s32[]{:S(2)}) async-start(), calls=%async_computation.7 | async-start | bytes 1310720 | tf_op jit(solution)/shard_map/all_gather | solution.py:48
  10.4 103.6 %all-gather.9.cloned.1.call-start = ((), (), s32[]{:S(2)}) async-start(), calls=%async_computation.6 | async-start | bytes 1310720 | tf_op jit(solution)/shard_map/all_gather | solution.py:48
  11.0 201.4 %reduce-scatter.11.cloned.1.call-start = ((), (), s32[]{:S(2)}) async-start(), calls=%async_computation.11 | async-start | bytes 1310720 | tf_op jit(solution)/shard_map/reduce_scatter | solution.py:139
  14.3 3.5 %copy-start.61 = (s32[4,64]{1,0:T(4,128)}, s32[4,64]{1,0:T(4,128)S(1)}, u32[]{:S(2)}) copy-start(s32[4,64]{1,0:T(4,128)S(1)} %eq.130) | copy-start | bytes 3076
  16.1 19.6 %copy-start.63 = (s32[4,64]{1,0:T(4,128)}, s32[4,64]{1,0:T(4,128)S(1)}, u32[]{:S(2)}) copy-start(s32[4,64]{1,0:T(4,128)S(1)} %slice.469) | copy-start | bytes 3076
  16.9 18.8 %copy-start.67 = (s32[4,64]{1,0:T(4,128)}, s32[4,64]{1,0:T(4,128)S(1)}, u32[]{:S(2)}) copy-start(s32[4,64]{1,0:T(4,128)S(1)} %slice.485) | copy-start | bytes 3076
  18.1 17.6 %copy-start.59 = (s32[8,128]{1,0:T(8,128)}, s32[8,128]{1,0:T(8,128)S(1)}, u32[]{:S(2)}) copy-start(s32[8,128]{1,0:T(8,128)S(1)} %reduce-window.9) | copy-start | bytes 12292
  18.3 17.4 %copy-start.93 = (s32[8]{0:T(128)}, s32[8]{0:T(128)S(1)}, u32[]{:S(2)}) copy-start(s32[8]{0:T(128)S(1)} %slice_reduce_fusion) | copy-start | bytes 100
  38.0 83.6 %copy-start.16 = (f32[4,64,256]{2,1,0:T(8,128)}, f32[4,64,256]{2,1,0:T(8,128)S(1)}, u32[]{:S(2)}) copy-start(f32[4,64,256]{2,1,0:T(8,128)S(1)} %reduce_window_sum.64) | copy-start | bytes 786436
  90.3 36.5 %copy-start.14 = (f32[4,64,256]{2,1,0:T(8,128)}, f32[4,64,256]{2,1,0:T(8,128)S(1)}, u32[]{:S(2)}) copy-start(f32[4,64,256]{2,1,0:T(8,128)S(1)} %reduce_window_sum.68) | copy-start | bytes 786436
  90.9 27.5 %copy-start.55 = (f32[4,1,256]{2,0,1:T(4,128)}, f32[4,1,256]{2,0,1:T(4,128)S(1)}, u32[]{:S(2)}) copy-start(f32[4,1,256]{2,0,1:T(4,128)S(1)} %copy.57) | copy-start | bytes 12292
  116.3 7.9 %copy-start.12 = (f32[4,64,256]{2,1,0:T(8,128)}, f32[4,64,256]{2,1,0:T(8,128)S(1)}, u32[]{:S(2)}) copy-start(f32[4,64,256]{2,1,0:T(8,128)S(1)} %reduce_window_sum.67) | copy-start | bytes 786436
  116.9 2.6 copy-start.57
  118.4 2.5 copy-start.100
  128.6 2.1 copy-start.19
  130.8 3.8 %copy-start.96 = (f32[1,256]{1,0:T(1,128)S(1)}, f32[1,256]{1,0:T(1,128)}, u32[]{:S(2)}) copy-start(f32[1,256]{1,0:T(1,128)} %get-tuple-element.90) | copy-start | bytes 3076
  134.6 18.7 %copy-start.73 = (f32[4,1,256]{2,1,0:T(1,128)S(1)}, f32[4,1,256]{2,1,0:T(1,128)}, u32[]{:S(2)}) copy-start(f32[4,1,256]{2,1,0:T(1,128)} %get-tuple-element.80) | copy-start | bytes 12292
  134.7 18.7 %copy-start.2 = (bf16[2048,256]{1,0:T(8,128)(2,1)S(1)}, bf16[2048,256]{1,0:T(8,128)(2,1)}, u32[]{:S(2)}) copy-start(bf16[2048,256]{1,0:T(8,128)(2,1)} %param.19) | copy-start | bytes 3145732
  136.2 19.6 %copy-start.68 = (s32[4,64]{1,0:T(4,128)S(1)}, s32[4,64]{1,0:T(4,128)}, u32[]{:S(2)}) copy-start(s32[4,64]{1,0:T(4,128)} %copy-done.67) | copy-start | bytes 3076
  138.6 17.2 %copy-start.15 = (f32[4,64,256]{2,1,0:T(8,128)S(1)}, f32[4,64,256]{2,1,0:T(8,128)}, u32[]{:S(2)}) copy-start(f32[4,64,256]{2,1,0:T(8,128)} %copy-done.14) | copy-start | bytes 786436
  138.6 17.2 %copy-start.24 = (bf16[256,256]{1,0:T(8,128)(2,1)S(1)}, bf16[256,256]{1,0:T(8,128)(2,1)}, u32[]{:S(2)}) copy-start(bf16[256,256]{1,0:T(8,128)(2,1)} %copy-done.23) | copy-start | bytes 393220
  139.6 16.6 %copy-start.46 = (f32[1,256,512]{2,1,0:T(8,128)S(1)}, f32[1,256,512]{2,1,0:T(8,128)}, u32[]{:S(2)}) copy-start(f32[1,256,512]{2,1,0:T(8,128)} %get-tuple-element.45) | copy-start | bytes 1572868
  139.7 16.6 %copy-start.47 = (f32[1,256,512]{2,1,0:T(8,128)S(1)}, f32[1,256,512]{2,1,0:T(8,128)}, u32[]{:S(2)}) copy-start(f32[1,256,512]{2,1,0:T(8,128)} %get-tuple-element.46) | copy-start | bytes 1572868
  139.7 16.6 %copy-start.48 = (f32[1,256,512]{2,1,0:T(8,128)S(1)}, f32[1,256,512]{2,1,0:T(8,128)}, u32[]{:S(2)}) copy-start(f32[1,256,512]{2,1,0:T(8,128)} %get-tuple-element.47) | copy-start | bytes 1572868
  139.7 16.6 %copy-start.49 = (f32[1,256,512]{2,1,0:T(8,128)S(1)}, f32[1,256,512]{2,1,0:T(8,128)}, u32[]{:S(2)}) copy-start(f32[1,256,512]{2,1,0:T(8,128)} %get-tuple-element.48) | copy-start | bytes 1572868
  139.7 16.6 %copy-start.99 = (f32[4,64]{1,0:T(4,128)S(1)}, f32[4,64]{1,0:T(4,128)}, u32[]{:S(2)}) copy-start(f32[4,64]{1,0:T(4,128)} %get-tuple-element.83) | copy-start | bytes 3076
  139.7 19.2 %collective-permute-start.3 = (bf16[258,512]{1,0:T(8,128)(2,1)S(1)}, bf16[258,512]{1,0:T(8,128)(2,1)S(1)}, u32[]{:S(2)}, u32[]{:S(2)}) collective-permute-start(bf16[258,512]{1,0:T(8,128)(2,1)S(1)} %pad_maximum_fusion.1), channel_id=1, source_target_pairs={{0,16},{4,20},{8,24},{12,28},{16,32},{20,36},{24,40},{28,44},{32,4... | collective-permute-start | bytes 792584 | tf_op jit(solution)/shard_map/ppermute | solution.py:14
  144.9 14.7 %collective-permute-start.2 = (bf16[258,512]{1,0:T(8,128)(2,1)S(1)}, bf16[258,512]{1,0:T(8,128)(2,1)S(1)}, u32[]{:S(2)}, u32[]{:S(2)}) collective-permute-start(bf16[258,512]{1,0:T(8,128)(2,1)S(1)} %pad_maximum_fusion.1), channel_id=1, source_target_pairs={{0,12},{4,16},{8,20},{12,24},{16,28},{20,32},{24,36},{28,40},{32,4... | collective-permute-start | bytes 792584 | tf_op jit(solution)/shard_map/ppermute | solution.py:14
  146.2 16.0 %collective-permute-start.1 = (bf16[258,512]{1,0:T(8,128)(2,1)S(1)}, bf16[258,512]{1,0:T(8,128)(2,1)S(1)}, u32[]{:S(2)}, u32[]{:S(2)}) collective-permute-start(bf16[258,512]{1,0:T(8,128)(2,1)S(1)} %pad_maximum_fusion.1), channel_id=1, source_target_pairs={{0,8},{4,12},{8,16},{12,20},{16,24},{20,28},{24,32},{28,36},{32,40... | collective-permute-start | bytes 792584 | tf_op jit(solution)/shard_map/ppermute | solution.py:14
  148.8 16.0 %collective-permute-start = (bf16[258,512]{1,0:T(8,128)(2,1)S(1)}, bf16[258,512]{1,0:T(8,128)(2,1)S(1)}, u32[]{:S(2)}, u32[]{:S(2)}) collective-permute-start(bf16[258,512]{1,0:T(8,128)(2,1)S(1)} %pad_maximum_fusion.1), channel_id=1, source_target_pairs={{0,4},{4,8},{8,12},{12,16},{16,20},{20,24},{24,28},{28,32},{32,36}... | collective-permute-start | bytes 792584 | tf_op jit(solution)/shard_map/ppermute | solution.py:14
  156.3 11.7 %copy-start.60 = (s32[8,128]{1,0:T(8,128)S(1)}, s32[8,128]{1,0:T(8,128)}, u32[]{:S(2)}) copy-start(s32[8,128]{1,0:T(8,128)} %copy-done.59) | copy-start | bytes 12292
  156.3 11.7 %copy-start.94 = (s32[8]{0:T(128)S(1)}, s32[8]{0:T(128)}, u32[]{:S(2)}) copy-start(s32[8]{0:T(128)} %copy-done.93) | copy-start | bytes 100
  158.9 7.3 %copy-start.53 = (bf16[258,512]{1,0:T(8,128)(2,1)}, bf16[258,512]{1,0:T(8,128)(2,1)S(1)}, u32[]{:S(2)}) copy-start(bf16[258,512]{1,0:T(8,128)(2,1)S(1)} %collective-permute-done.3) | copy-start | bytes 792580
  168.1 3.9 %copy-start.54 = (bf16[258,512]{1,0:T(8,128)(2,1)S(1)}, bf16[258,512]{1,0:T(8,128)(2,1)}, u32[]{:S(2)}) copy-start(bf16[258,512]{1,0:T(8,128)(2,1)} %copy-done.53) | copy-start | bytes 792580
  170.8 2.2 copy-start.18
  170.8 2.2 copy-start.34
  175.0 4.5 %copy-start.72 = (f32[4,1,256]{2,1,0:T(1,128)S(1)}, f32[4,1,256]{2,1,0:T(1,128)}, u32[]{:S(2)}) copy-start(f32[4,1,256]{2,1,0:T(1,128)} %get-tuple-element.78) | copy-start | bytes 12292
  179.4 51.9 %reduce-scatter.9.cloned.1.call-start = ((), (), s32[]{:S(2)}) async-start(), calls=%async_computation.10 | async-start | bytes 1310720 | tf_op jit(solution)/shard_map/reduce_scatter | solution.py:139
  181.4 2.2 copy-start.22
  181.4 2.2 copy-start.66
  181.5 2.6 copy-start.31
  186.7 4.8 %copy-start.71 = (f32[4,1,256]{2,1,0:T(1,128)S(1)}, f32[4,1,256]{2,1,0:T(1,128)}, u32[]{:S(2)}) copy-start(f32[4,1,256]{2,1,0:T(1,128)} %get-tuple-element.76) | copy-start | bytes 12292
  191.2 66.1 %reduce-scatter.7.cloned.1.call-start = ((), (), s32[]{:S(2)}) async-start(), calls=%async_computation.9 | async-start | bytes 1310720 | tf_op jit(solution)/shard_map/reduce_scatter | solution.py:139
  193.3 2.2 copy-start.20
  193.3 2.2 copy-start.64
  193.4 2.6 copy-start.29
  196.0 2.0 copy-start.102
  198.0 4.5 %copy-start.70 = (f32[4,1,256]{2,1,0:T(1,128)S(1)}, f32[4,1,256]{2,1,0:T(1,128)}, u32[]{:S(2)}) copy-start(f32[4,1,256]{2,1,0:T(1,128)} %get-tuple-element.74) | copy-start | bytes 12292
  202.5 2.0 copy-start.62
  202.5 80.7 %reduce-scatter.5.cloned.1.call-start = ((), (), s32[]{:S(2)}) async-start(), calls=%async_computation.8 | async-start | bytes 1310720 | tf_op jit(solution)/shard_map/reduce_scatter | solution.py:139
  202.5 2.4 copy-start.26
  202.6 2.8 copy-start.35
  202.6 2.8 copy-start.36
  202.6 2.8 copy-start.37
  202.6 2.8 copy-start.98
  205.4 2.9 %copy-start.8 = (bf16[256,2048]{1,0:T(8,128)(2,1)S(1)}, bf16[256,2048]{1,0:T(8,128)(2,1)}, u32[]{:S(2)}) copy-start(bf16[256,2048]{1,0:T(8,128)(2,1)} %all-gather.5.cloned.1.call-done) | copy-start | bytes 3145732
  205.4 2.9 copy-start.103
  (53 other events, 75.1 us)
Sparse Core Ops, SparseCore 0:
  9.1 26.5 all-gather.4
  37.4 24.4 all-gather.6
  63.5 24.4 all-gather.10
  89.5 24.4 all-gather.8
  179.5 25.9 reduce-scatter.10
  207.8 23.4 reduce-scatter.8
  233.7 23.4 reduce-scatter.6
  259.6 23.4 reduce-scatter.4
where the time goes:
time: 293 us; the launch traced here: 292 us
  waiting for transfers between devices  157 us (54%)
  matrix products  59.7 us (20%)
  between operations  21.6 us (7%)
  local copies, waits for them, and re-layouts  21.5 us (7%)
  other arithmetic  18.3 us (6%)
  starting transfers between devices  14.2 us (5%)
    all_gather x4, waiting for transfers between devices, body(): piece = lax.all_gather(hidden_in[rows], 'tensor', axis=1, tiled=True)  84.2 us
    reduce_scatter x4, waiting for transfers between devices, body(): lax.psum_scatter(head_term.astype(jnp.bfloat16), 'tensor', scatter_dimens...  70.7 us
    dot_general x16, matrix products, body(): jnp.dot(piece, weight, preferred_element_type=jnp.float32)  19 us
    dot_general x4, matrix products, body(): head_term = jnp.dot(gated, w_out, preferred_element_type=jnp.float32)  17.3 us
    ppermute x4, starting transfers between devices, shifted(): return lax.ppermute(x, axis, pairs)  13.6 us
    dot_general x4, matrix products, body(): jnp.einsum('ncd,ndv->ncv', q_float * jnp.exp(cumul), jnp.stack(states), p...  7.03 us
  transfers between devices with their start and end apart: 12, of which 7 were waited for; matrix products, arithmetic and copies ran while one was open for 19% of the time, Pallas kernels for 0%

commit v1 on v0

--- a/solution.py
+++ b/solution.py
@@ -45,7 +45,10 @@
     parts = []
     for p in range(PIECES):
         rows = slice(p * piece_rows, (p + 1) * piece_rows)
-        piece = lax.all_gather(hidden_in[rows], "tensor", axis=1, tiled=True)
+        piece = jnp.concatenate(
+            lax.all_to_all(jnp.stack([hidden_in[rows]] * lax.axis_size("tensor")), "tensor", 0, 0),
+            axis=1,
+        )
         query_sum, key_sum, value_sum, outgate, low = tuple(
             (jnp.dot(piece, weight, preferred_element_type=jnp.float32) for weight in weights)
         )

time: 293 us -> 281 us (0.959)
  waiting for transfers between devices: 157 us -> 94.9 us
  starting transfers between devices: 14.2 us -> 32.3 us
  matrix products: 59.7 us -> 75 us
  local copies, waits for them, and re-layouts: 21.5 us -> 34.2 us
  other arithmetic: 18.3 us -> 22.4 us
    all_gather x4 -> x0, waiting for transfers between devices: 84.2 us -> none  [body(): piece = lax.all_gather(hidden_in[rows], 'tensor', axis=1, tiled=True)]
    all_to_all x0 -> x4, waiting for transfers between devices: none -> 22.9 us  [body(): lax.all_to_all(jnp.stack([hidden_in[rows]] * lax.axis_size('tensor')), 't...]
    all_to_all x0 -> x4, starting transfers between devices: none -> 17.4 us  [body(): lax.all_to_all(jnp.stack([hidden_in[rows]] * lax.axis_size('tensor')), 't...]
    dot_general x16, matrix products: 19 us -> 34.1 us  [body(): jnp.dot(piece, weight, preferred_element_type=jnp.float32)]
    another operation x2 -> x6, local copies, waits for them, and re-layouts: 0.19 us -> 6.24 us  [the longest x4 6.05 us: body(): jnp.stack([hidden_in[rows]] * lax.axis_size('tensor'))]
    slice x1 -> x5, local copies, waits for them, and re-layouts: 2.32 us -> 6.09 us  [body(): hidden_in[rows]]
    squeeze x0 -> x3, local copies, waits for them, and re-layouts: none -> 3.16 us  [body(): block_totals = cumul[:, -1, :]]
  transfers between devices with their start and end apart: 12 -> 12, of which waited for: 7 -> 8; matrix products, arithmetic and copies ran while one was open for 19% -> 24% of each run, Pallas kernels for 0% -> 0%
where the time goes in v1:
time: 281 us; the launch traced here: 280 us
  waiting for transfers between devices  94.9 us (34%)
  matrix products  75 us (27%)
  local copies, waits for them, and re-layouts  34.2 us (12%)
  starting transfers between devices  32.3 us (11%)
  other arithmetic  22.4 us (8%)
  between operations  21 us (7%)
    reduce_scatter x4, waiting for transfers between devices, body(): lax.psum_scatter(head_term.astype(jnp.bfloat16), 'tensor', scatter_dimens...  71.6 us
    dot_general x16, matrix products, body(): jnp.dot(piece, weight, preferred_element_type=jnp.float32)  34.1 us
    all_to_all x4, waiting for transfers between devices, body(): lax.all_to_all(jnp.stack([hidden_in[rows]] * lax.axis_size('tensor')), 't...  22.9 us
    dot_general x4, matrix products, body(): head_term = jnp.dot(gated, w_out, preferred_element_type=jnp.float32)  17.6 us
    all_to_all x4, starting transfers between devices, body(): lax.all_to_all(jnp.stack([hidden_in[rows]] * lax.axis_size('tensor')), 't...  17.4 us
    ppermute x4, starting transfers between devices, shifted(): return lax.ppermute(x, axis, pairs)  14.2 us
    dot_general x4, matrix products, body(): jnp.einsum('ncd,ndv->ncv', q_float * jnp.exp(cumul), jnp.stack(states), p...  6.25 us
    slice x5, local copies, waits for them, and re-layouts, body(): hidden_in[rows]  6.09 us
  transfers between devices with their start and end apart: 12, of which 8 were waited for; matrix products, arithmetic and copies ran while one was open for 24% of the time, Pallas kernels for 0%

profile of v1, /device:TPU:0, one launch (start us, length us, event | category | flops | bytes accessed | tf_op | source)
XLA Modules:
  0.0 279.7 jit_solution(17986343779974665119)
XLA Ops:
  6.5 2.2 fusion.172
  8.9 1.0 stack.19
  10.0 4.6 %all-to-all-start.2 = ((bf16[4,256,512]{1,2,0:T(8,128)(2,1)}), bf16[4,256,512]{1,2,0:T(8,128)(2,1)S(1)}, u32[]{:S(2)}, u32[]{:S(2)}) async-start(bf16[4,256,512]{1,2,0:T(8,128)(2,1)} %stack.19), calls=%async_computation.2 | async-start | bytes 2097152 | tf_op jit(solution)/shard_map/all_to_all | solution.py:49
  17.8 1.1 copy.37
  21.0 8.6 %all-to-all-done.2 = bf16[4,256,512]{1,2,0:T(8,128)(2,1)S(1)} async-done(((bf16[4,256,512]{1,2,0:T(8,128)(2,1)}), bf16[4,256,512]{1,2,0:T(8,128)(2,1)S(1)}, u32[]{:S(2)}, u32[]{:S(2)}) %all-to-all-start.2) | async-done | bytes 1048608 | tf_op jit(solution)/shard_map/all_to_all | solution.py:49
  31.6 4.4 %all-to-all-start.3 = ((bf16[4,256,512]{1,2,0:T(8,128)(2,1)}), bf16[4,256,512]{1,2,0:T(8,128)(2,1)}, u32[]{:S(2)}, u32[]{:S(2)}) async-start(bf16[4,256,512]{1,2,0:T(8,128)(2,1)} %stack.20), calls=%async_computation.3 | async-start | bytes 2097152 | tf_op jit(solution)/shard_map/all_to_all | solution.py:49
  39.1 1.8 copy.34
  42.4 2.1 fusion.197
  44.4 1.7 convolution_convert_fusion.12
  46.2 4.2 %all-to-all-done.3 = bf16[4,256,512]{1,2,0:T(8,128)(2,1)} async-done(((bf16[4,256,512]{1,2,0:T(8,128)(2,1)}), bf16[4,256,512]{1,2,0:T(8,128)(2,1)}, u32[]{:S(2)}, u32[]{:S(2)}) %all-to-all-start.3) | async-done | bytes 1048608 | tf_op jit(solution)/shard_map/all_to_all | solution.py:49
  50.3 2.0 stack.18
  52.3 4.2 %all-to-all-start.1 = ((bf16[4,256,512]{1,2,0:T(8,128)(2,1)}), bf16[4,256,512]{1,2,0:T(8,128)(2,1)}, u32[]{:S(2)}, u32[]{:S(2)}) async-start(bf16[4,256,512]{1,2,0:T(8,128)(2,1)} %stack.18), calls=%async_computation.1 | async-start | bytes 2097152 | tf_op jit(solution)/shard_map/all_to_all | solution.py:49
  56.6 2.2 fusion.198
  58.8 2.4 convolution_convert_fusion.11
  61.2 1.4 convolution_convert_fusion.5
  62.6 7.4 %all-to-all-done.1 = bf16[4,256,512]{1,2,0:T(8,128)(2,1)} async-done(((bf16[4,256,512]{1,2,0:T(8,128)(2,1)}), bf16[4,256,512]{1,2,0:T(8,128)(2,1)}, u32[]{:S(2)}, u32[]{:S(2)}) %all-to-all-start.1) | async-done | bytes 1048608 | tf_op jit(solution)/shard_map/all_to_all | solution.py:49
  70.0 2.0 stack.16
  72.0 4.2 %all-to-all-start = ((bf16[4,256,512]{1,2,0:T(8,128)(2,1)}), bf16[4,256,512]{1,2,0:T(8,128)(2,1)}, u32[]{:S(2)}, u32[]{:S(2)}) async-start(bf16[4,256,512]{1,2,0:T(8,128)(2,1)} %stack.16), calls=%async_computation | async-start | bytes 2097152 | tf_op jit(solution)/shard_map/all_to_all | solution.py:49
  76.5 1.9 convolution_convert_fusion.13
  78.3 2.1 fusion.196
  80.5 2.7 convolution_convert_fusion.4
  83.1 2.7 convolution_convert_fusion.6
  85.8 2.7 all-to-all-done
  88.5 2.2 fusion.195
  90.7 1.7 convolution_convert_fusion.14
  92.5 2.7 convolution_convert_fusion.7
  97.9 1.2 fusion.96
  99.3 1.3 copy_bitcast_fusion.1
  103.2 1.9 fusion.94
  105.1 1.2 reduce_window_sum.64
  106.3 1.3 copy_bitcast_fusion
  110.8 1.3 reduce_window_sum.69
  114.7 1.2 fusion.82
  115.9 1.2 fusion.88
  117.1 1.2 fusion.91
  118.5 1.2 fusion.85
  119.8 3.6 %multiply_add_fusion = (f32[1,256,512]{2,1,0:T(8,128)}, f32[1,256,512]{2,1,0:T(8,128)}, f32[1,256,512]{2,1,0:T(8,128)}, f32[1,256,512]{2,1,0:T(8,128)}, f32[1,25...) fusion(f32[4,256,512]{2,1,0:T(8,128)S(1)} %fusion.91, ...), kind=kLoop, calls=%fused_computation.127 | loop fusion | flops 3801088 | bytes 15744000 | tf_op jit(solution)/shard_map/add | solution.py:99
  123.5 1.5 fusion.65
  125.0 1.3 scatter.11
  126.3 1.4 scatter.14
  128.7 5.9 %collective-permute-start.3 = (bf16[258,512]{1,0:T(8,128)(2,1)S(1)}, bf16[258,512]{1,0:T(8,128)(2,1)S(1)}, u32[]{:S(2)}, u32[]{:S(2)}) collective-permute-start(bf16[258,512]{1,0:T(8,128)(2,1)S(1)} %pad_maximum_fusion.1), channel_id=1, source_target_pairs={{0,16},{4,20},{8,24},{12,28},{16,32},{20,36},{24,40},{28,44},{32,4... | collective-permute-start | bytes 792584 | tf_op jit(solution)/shard_map/ppermute | solution.py:14
  134.6 1.3 collective-permute-start.2
  136.0 2.9 %collective-permute-start.1 = (bf16[258,512]{1,0:T(8,128)(2,1)S(1)}, bf16[258,512]{1,0:T(8,128)(2,1)S(1)}, u32[]{:S(2)}, u32[]{:S(2)}) collective-permute-start(bf16[258,512]{1,0:T(8,128)(2,1)S(1)} %pad_maximum_fusion.1), channel_id=1, source_target_pairs={{0,8},{4,12},{8,16},{12,20},{16,24},{20,28},{24,32},{28,36},{32,40... | collective-permute-start | bytes 792584 | tf_op jit(solution)/shard_map/ppermute | solution.py:14
  138.9 4.0 %collective-permute-start = (bf16[258,512]{1,0:T(8,128)(2,1)S(1)}, bf16[258,512]{1,0:T(8,128)(2,1)S(1)}, u32[]{:S(2)}, u32[]{:S(2)}) collective-permute-start(bf16[258,512]{1,0:T(8,128)(2,1)S(1)} %pad_maximum_fusion.1), channel_id=1, source_target_pairs={{0,4},{4,8},{8,12},{12,16},{16,20},{20,24},{24,28},{28,32},{32,36}... | collective-permute-start | bytes 792584 | tf_op jit(solution)/shard_map/ppermute | solution.py:14
  143.0 2.5 bitcast_multiply_fusion
  146.0 1.4 fusion.31
  159.9 1.0 convert_element_type.186
  161.3 1.5 multiply_reduce_fusion
  163.3 4.5 %convolution_convert_fusion = bf16[256,2048]{1,0:T(8,128)(2,1)} fusion(bf16[512,2048]{1,0:T(8,128)(2,1)S(1)} %copy-done, f32[256,512]{1,0:T(8,128)} %get-tuple-element.117, f32[256]{0:T(256)} %rsqrt_multiply_fusion, f32[512]{0:T(512)} %param.26, bf16[256,2048]{0,1:T(8,128)(2,1)} %bitcast.19, bf16[2048,512]{1,0:T(8,128)(2,1)} %param.22), kind=kOutput, calls=%fused_computation | convolution fusion | flops 1075314688 | bytes 6818816 | tf_op jit(solution)/shard_map/dot_general | solution.py:140
  167.9 1.9 bitcast_multiply_fusion.1
  169.9 2.1 fusion.34
  173.0 1.5 multiply_reduce_fusion.1
  174.5 4.2 %convolution_convert_fusion.1 = bf16[256,2048]{1,0:T(8,128)(2,1)} fusion(bf16[512,2048]{1,0:T(8,128)(2,1)S(1)} %copy-done, f32[256,512]{1,0:T(8,128)} %get-tuple-element.121, f32[256]{0:T(256)S(1)} %rsqrt_multiply_fusion.1, f32[512]{0:T(512)} %param.26, bf16[256,2048]{0,1:T(8,128)(2,1)S(1)} %bitcast.281, bf16[2048,512]{1,0:T(8,128)(2,1)} %param.22), kind=kOutput, calls=%fused_computation.1 | convolution fusion | flops 1075314688 | bytes 6818816 | tf_op jit(solution)/shard_map/dot_general | solution.py:140
  179.0 2.2 bitcast_multiply_fusion.2
  181.3 1.4 fusion.37
  183.8 1.5 multiply_reduce_fusion.2
  185.2 4.6 %convolution_convert_fusion.2 = bf16[256,2048]{1,0:T(8,128)(2,1)} fusion(bf16[512,2048]{1,0:T(8,128)(2,1)S(1)} %copy-done, f32[256,512]{1,0:T(8,128)} %get-tuple-element.125, f32[256]{0:T(256)S(1)} %rsqrt_multiply_fusion.2, f32[512]{0:T(512)S(1)} %copy-done.105, bf16[256,2048]{0,1:T(8,128)(2,1)} %bitcast.13, bf16[2048,512]{1,0:T(8,128)(2,1)} %param.22), kind=kOutput, calls=%fused_computation.2 | convolution fusion | flops 1075314688 | bytes 6818816 | tf_op jit(solution)/shard_map/dot_general | solution.py:140
  189.9 1.9 bitcast_multiply_fusion.3
  192.8 1.4 fusion.43
  195.0 4.4 %convolution_convert_fusion.3 = bf16[256,2048]{1,0:T(8,128)(2,1)} fusion(bf16[512,2048]{1,0:T(8,128)(2,1)S(1)} %copy-done, f32[256,512]{1,0:T(8,128)S(1)} %get-tuple-element.129, f32[512]{0:T(512)S(1)} %copy-done.106, f32[256]{0:T(256)S(1)} %rsqrt_multiply_fusion.3, bf16[256,2048]{0,1:T(8,128)(2,1)} %bitcast.1, bf16[2048,512]{1,0:T(8,128)(2,1)} %param.22), kind=kOutput, calls=%fused_computation.3 | convolution fusion | flops 1075314688 | bytes 6818816 | tf_op jit(solution)/shard_map/dot_general | solution.py:140
  199.4 20.0 %reduce-scatter.9.cloned.1.call-done = bf16[256,512]{1,0:T(8,128)(2,1)} async-done(((bf16[256,2048]{1,0:T(8,128)(2,1)}), bf16[256,512]{1,0:T(8,128)(2,1)}) %reduce-scatter.9.cloned.1.call-update) | async-done | bytes 262160 | tf_op jit(solution)/shard_map/reduce_scatter | solution.py:142
  219.4 25.9 %reduce-scatter.7.cloned.1.call-done = bf16[256,512]{1,0:T(8,128)(2,1)} async-done(((bf16[256,2048]{1,0:T(8,128)(2,1)}), bf16[256,512]{1,0:T(8,128)(2,1)}) %reduce-scatter.7.cloned.1.call-update) | async-done | bytes 262160 | tf_op jit(solution)/shard_map/reduce_scatter | solution.py:142
  245.3 25.7 %reduce-scatter.5.cloned.1.call-done = bf16[256,512]{1,0:T(8,128)(2,1)} async-done(((bf16[256,2048]{1,0:T(8,128)(2,1)}), bf16[256,512]{1,0:T(8,128)(2,1)}) %reduce-scatter.5.cloned.1.call-update) | async-done | bytes 262160 | tf_op jit(solution)/shard_map/reduce_scatter | solution.py:142
  270.9 2.2 pad_maximum_fusion
  (311 shorter events, 36.2 us)
Async XLA Ops:
  6.5 156.7 %copy-start = (bf16[512,2048]{1,0:T(8,128)(2,1)S(1)}, bf16[512,2048]{1,0:T(8,128)(2,1)}, u32[]{:S(2)}) copy-start(bf16[512,2048]{1,0:T(8,128)(2,1)} %param.27) | copy-start | bytes 6291460
  8.8 5.8 %copy-start.68 = (s32[1024]{0:T(1024)S(1)}, s32[1024]{0:T(1024)}, u32[]{:S(2)}) copy-start(s32[1024]{0:T(1024)} %param.18) | copy-start | bytes 12292
  10.0 19.7 %all-to-all-start.2 = ((bf16[4,256,512]{1,2,0:T(8,128)(2,1)}), bf16[4,256,512]{1,2,0:T(8,128)(2,1)S(1)}, u32[]{:S(2)}, u32[]{:S(2)}) async-start(bf16[4,256,512]{1,2,0:T(8,128)(2,1)} %stack.19), calls=%async_computation.2 | async-start | bytes 2097152 | tf_op jit(solution)/shard_map/all_to_all | solution.py:49
  14.7 3.1 %copy-start.60 = (s32[4,64]{1,0:T(4,128)}, s32[4,64]{1,0:T(4,128)S(1)}, u32[]{:S(2)}) copy-start(s32[4,64]{1,0:T(4,128)S(1)} %eq.130) | copy-start | bytes 3076
  16.5 24.4 %copy-start.62 = (s32[4,64]{1,0:T(4,128)}, s32[4,64]{1,0:T(4,128)S(1)}, u32[]{:S(2)}) copy-start(s32[4,64]{1,0:T(4,128)S(1)} %slice.469) | copy-start | bytes 3076
  16.7 24.1 %copy-start.66 = (s32[4,64]{1,0:T(4,128)}, s32[4,64]{1,0:T(4,128)S(1)}, u32[]{:S(2)}) copy-start(s32[4,64]{1,0:T(4,128)S(1)} %slice.485) | copy-start | bytes 3076
  17.1 23.8 %copy-start.58 = (s32[8,128]{1,0:T(8,128)}, s32[8,128]{1,0:T(8,128)S(1)}, u32[]{:S(2)}) copy-start(s32[8,128]{1,0:T(8,128)S(1)} %reduce-window.9) | copy-start | bytes 12292
  17.3 23.6 %copy-start.94 = (s32[8]{0:T(128)}, s32[8]{0:T(128)S(1)}, u32[]{:S(2)}) copy-start(s32[8]{0:T(128)S(1)} %slice_reduce_fusion) | copy-start | bytes 100
  21.0 21.3 %copy-start.25 = (bf16[2048,16]{0,1:T(8,128)(2,1)S(1)}, bf16[2048,16]{0,1:T(8,128)(2,1)}, u32[]{:S(2)}) copy-start(bf16[2048,16]{0,1:T(8,128)(2,1)} %param.23) | copy-start | bytes 196612
  31.6 9.3 %copy-start.32 = (bf16[256,512]{1,0:T(8,128)(2,1)S(1)}, bf16[256,512]{1,0:T(8,128)(2,1)}, u32[]{:S(2)}) copy-start(bf16[256,512]{1,0:T(8,128)(2,1)} %get-tuple-element.65) | copy-start | bytes 786436
  31.6 12.8 %copy-start.1 = (bf16[2048,256]{1,0:T(8,128)(2,1)S(1)}, bf16[2048,256]{1,0:T(8,128)(2,1)}, u32[]{:S(2)}) copy-start(bf16[2048,256]{1,0:T(8,128)(2,1)} %param.20) | copy-start | bytes 3145732
  31.6 18.7 %all-to-all-start.3 = ((bf16[4,256,512]{1,2,0:T(8,128)(2,1)}), bf16[4,256,512]{1,2,0:T(8,128)(2,1)}, u32[]{:S(2)}, u32[]{:S(2)}) async-start(bf16[4,256,512]{1,2,0:T(8,128)(2,1)} %stack.20), calls=%async_computation.3 | async-start | bytes 2097152 | tf_op jit(solution)/shard_map/all_to_all | solution.py:49
  46.1 69.7 %copy-start.19 = (bf16[256,256]{1,0:T(8,128)(2,1)}, bf16[256,256]{1,0:T(8,128)(2,1)S(1)}, u32[]{:S(2)}) copy-start(bf16[256,256]{1,0:T(8,128)(2,1)S(1)} %convolution_convert_fusion.12) | copy-start | bytes 393220
  52.3 17.7 %all-to-all-start.1 = ((bf16[4,256,512]{1,2,0:T(8,128)(2,1)}), bf16[4,256,512]{1,2,0:T(8,128)(2,1)}, u32[]{:S(2)}, u32[]{:S(2)}) async-start(bf16[4,256,512]{1,2,0:T(8,128)(2,1)} %stack.18), calls=%async_computation.1 | async-start | bytes 2097152 | tf_op jit(solution)/shard_map/all_to_all | solution.py:49
  56.6 4.6 %copy-start.3 = (bf16[4,256,512]{1,2,0:T(8,128)(2,1)S(1)}, bf16[4,256,512]{1,2,0:T(8,128)(2,1)}, u32[]{:S(2)}) copy-start(bf16[4,256,512]{1,2,0:T(8,128)(2,1)} %copy-done.2) | copy-start | bytes 3145732
  56.6 4.6 %copy-start.101 = (bf16[2048,512]{1,0:T(8,128)(2,1)S(1)}, bf16[2048,512]{1,0:T(8,128)(2,1)}, u32[]{:S(2)}) copy-start(bf16[2048,512]{1,0:T(8,128)(2,1)} %param.21) | copy-start | bytes 6291460
  72.0 16.5 %all-to-all-start = ((bf16[4,256,512]{1,2,0:T(8,128)(2,1)}), bf16[4,256,512]{1,2,0:T(8,128)(2,1)}, u32[]{:S(2)}, u32[]{:S(2)}) async-start(bf16[4,256,512]{1,2,0:T(8,128)(2,1)} %stack.16), calls=%async_computation | async-start | bytes 2097152 | tf_op jit(solution)/shard_map/all_to_all | solution.py:49
  76.2 123.1 %reduce-scatter.11.cloned.1.call-start = ((), (), s32[]{:S(2)}) async-start(), calls=%async_computation.11 | async-start | bytes 1310720 | tf_op jit(solution)/shard_map/reduce_scatter | solution.py:142
  76.5 4.0 %copy-start.102 = (bf16[2048,512]{1,0:T(8,128)(2,1)S(1)}, bf16[2048,512]{1,0:T(8,128)(2,1)}, u32[]{:S(2)}) copy-start(bf16[2048,512]{1,0:T(8,128)(2,1)} %param.21) | copy-start | bytes 6291460
  78.3 40.1 %copy-start.17 = (bf16[256,256]{1,0:T(8,128)(2,1)}, bf16[256,256]{1,0:T(8,128)(2,1)S(1)}, u32[]{:S(2)}) copy-start(bf16[256,256]{1,0:T(8,128)(2,1)S(1)} %convolution_convert_fusion.13) | copy-start | bytes 393220
  88.5 3.9 %copy-start.103 = (bf16[2048,512]{1,0:T(8,128)(2,1)S(1)}, bf16[2048,512]{1,0:T(8,128)(2,1)}, u32[]{:S(2)}) copy-start(bf16[2048,512]{1,0:T(8,128)(2,1)} %param.21) | copy-start | bytes 6291460
  92.5 2.7 copy-start.73
  92.5 2.7 copy-start.104
  92.5 2.7 copy-start.107
  92.5 4.0 %copy-start.74 = (f32[256,16]{0,1:T(8,128)S(1)}, f32[256,16]{0,1:T(8,128)}, u32[]{:S(2)}) copy-start(f32[256,16]{0,1:T(8,128)} %fusion.198) | copy-start | bytes 49156
  95.9 19.9 %copy-start.11 = (f32[4,64,256]{2,1,0:T(8,128)}, f32[4,64,256]{2,1,0:T(8,128)S(1)}, u32[]{:S(2)}) copy-start(f32[4,64,256]{2,1,0:T(8,128)S(1)} %reduce_window_sum.67) | copy-start | bytes 786436
  97.2 19.8 %copy-start.13 = (f32[4,64,256]{2,1,0:T(8,128)}, f32[4,64,256]{2,1,0:T(8,128)S(1)}, u32[]{:S(2)}) copy-start(f32[4,64,256]{2,1,0:T(8,128)S(1)} %reduce_window_sum.68) | copy-start | bytes 786436
  106.3 8.3 %copy-start.15 = (f32[4,64,256]{2,1,0:T(8,128)}, f32[4,64,256]{2,1,0:T(8,128)S(1)}, u32[]{:S(2)}) copy-start(f32[4,64,256]{2,1,0:T(8,128)S(1)} %reduce_window_sum.64) | copy-start | bytes 786436
  107.6 2.6 copy-start.54
  112.9 2.9 %copy-start.28 = (bf16[256,512]{1,0:T(8,128)(2,1)S(1)}, bf16[256,512]{1,0:T(8,128)(2,1)}, u32[]{:S(2)}) copy-start(bf16[256,512]{1,0:T(8,128)(2,1)} %convolution_convert_fusion.5) | copy-start | bytes 786436
  113.0 2.9 %copy-start.91 = (f32[4,64]{1,0:T(4,128)S(1)}, f32[4,64]{1,0:T(4,128)}, u32[]{:S(2)}) copy-start(f32[4,64]{1,0:T(4,128)} %compare_convert_fusion.2) | copy-start | bytes 3076
  115.9 2.6 copy-start.26
  115.9 2.6 copy-start.92
  119.8 3.6 %copy-start.97 = (f32[1,256]{1,0:T(1,128)S(1)}, f32[1,256]{1,0:T(1,128)}, u32[]{:S(2)}) copy-start(f32[1,256]{1,0:T(1,128)} %get-tuple-element.90) | copy-start | bytes 3076
  123.5 19.5 %copy-start.5 = (bf16[2048,256]{1,0:T(8,128)(2,1)S(1)}, bf16[2048,256]{1,0:T(8,128)(2,1)}, u32[]{:S(2)}) copy-start(bf16[2048,256]{1,0:T(8,128)(2,1)} %param.19) | copy-start | bytes 3145732
  125.0 20.5 %copy-start.67 = (s32[4,64]{1,0:T(4,128)S(1)}, s32[4,64]{1,0:T(4,128)}, u32[]{:S(2)}) copy-start(s32[4,64]{1,0:T(4,128)} %copy-done.66) | copy-start | bytes 3076
  125.0 20.5 %copy-start.72 = (f32[4,256]{1,0:T(4,128)S(1)}, f32[4,256]{1,0:T(4,128)}, u32[]{:S(2)}) copy-start(f32[4,256]{1,0:T(4,128)} %get-tuple-element.137) | copy-start | bytes 12292
  127.6 17.8 %copy-start.14 = (f32[4,64,256]{2,1,0:T(8,128)S(1)}, f32[4,64,256]{2,1,0:T(8,128)}, u32[]{:S(2)}) copy-start(f32[4,64,256]{2,1,0:T(8,128)} %copy-done.13) | copy-start | bytes 786436
  127.6 17.8 %copy-start.22 = (bf16[256,256]{1,0:T(8,128)(2,1)S(1)}, bf16[256,256]{1,0:T(8,128)(2,1)}, u32[]{:S(2)}) copy-start(bf16[256,256]{1,0:T(8,128)(2,1)} %convolution_convert_fusion.11) | copy-start | bytes 393220
  128.6 17.3 %copy-start.45 = (f32[1,256,512]{2,1,0:T(8,128)S(1)}, f32[1,256,512]{2,1,0:T(8,128)}, u32[]{:S(2)}) copy-start(f32[1,256,512]{2,1,0:T(8,128)} %get-tuple-element.45) | copy-start | bytes 1572868
  128.7 17.3 %copy-start.46 = (f32[1,256,512]{2,1,0:T(8,128)S(1)}, f32[1,256,512]{2,1,0:T(8,128)}, u32[]{:S(2)}) copy-start(f32[1,256,512]{2,1,0:T(8,128)} %get-tuple-element.46) | copy-start | bytes 1572868
  128.7 17.3 %copy-start.47 = (f32[1,256,512]{2,1,0:T(8,128)S(1)}, f32[1,256,512]{2,1,0:T(8,128)}, u32[]{:S(2)}) copy-start(f32[1,256,512]{2,1,0:T(8,128)} %get-tuple-element.47) | copy-start | bytes 1572868
  128.7 17.3 %copy-start.48 = (f32[1,256,512]{2,1,0:T(8,128)S(1)}, f32[1,256,512]{2,1,0:T(8,128)}, u32[]{:S(2)}) copy-start(f32[1,256,512]{2,1,0:T(8,128)} %get-tuple-element.48) | copy-start | bytes 1572868
  128.7 17.3 %copy-start.100 = (f32[4,64]{1,0:T(4,128)S(1)}, f32[4,64]{1,0:T(4,128)}, u32[]{:S(2)}) copy-start(f32[4,64]{1,0:T(4,128)} %get-tuple-element.83) | copy-start | bytes 3076
  128.7 19.1 %collective-permute-start.3 = (bf16[258,512]{1,0:T(8,128)(2,1)S(1)}, bf16[258,512]{1,0:T(8,128)(2,1)S(1)}, u32[]{:S(2)}, u32[]{:S(2)}) collective-permute-start(bf16[258,512]{1,0:T(8,128)(2,1)S(1)} %pad_maximum_fusion.1), channel_id=1, source_target_pairs={{0,16},{4,20},{8,24},{12,28},{16,32},{20,36},{24,40},{28,44},{32,4... | collective-permute-start | bytes 792584 | tf_op jit(solution)/shard_map/ppermute | solution.py:14
  134.6 13.7 %collective-permute-start.2 = (bf16[258,512]{1,0:T(8,128)(2,1)S(1)}, bf16[258,512]{1,0:T(8,128)(2,1)S(1)}, u32[]{:S(2)}, u32[]{:S(2)}) collective-permute-start(bf16[258,512]{1,0:T(8,128)(2,1)S(1)} %pad_maximum_fusion.1), channel_id=1, source_target_pairs={{0,12},{4,16},{8,20},{12,24},{16,28},{20,32},{24,36},{28,40},{32,4... | collective-permute-start | bytes 792584 | tf_op jit(solution)/shard_map/ppermute | solution.py:14
  136.0 15.2 %collective-permute-start.1 = (bf16[258,512]{1,0:T(8,128)(2,1)S(1)}, bf16[258,512]{1,0:T(8,128)(2,1)S(1)}, u32[]{:S(2)}, u32[]{:S(2)}) collective-permute-start(bf16[258,512]{1,0:T(8,128)(2,1)S(1)} %pad_maximum_fusion.1), channel_id=1, source_target_pairs={{0,8},{4,12},{8,16},{12,20},{16,24},{20,28},{24,32},{28,36},{32,40... | collective-permute-start | bytes 792584 | tf_op jit(solution)/shard_map/ppermute | solution.py:14
  138.9 14.9 %collective-permute-start = (bf16[258,512]{1,0:T(8,128)(2,1)S(1)}, bf16[258,512]{1,0:T(8,128)(2,1)S(1)}, u32[]{:S(2)}, u32[]{:S(2)}) collective-permute-start(bf16[258,512]{1,0:T(8,128)(2,1)S(1)} %pad_maximum_fusion.1), channel_id=1, source_target_pairs={{0,4},{4,8},{8,12},{12,16},{16,20},{20,24},{24,28},{28,32},{32,36}... | collective-permute-start | bytes 792584 | tf_op jit(solution)/shard_map/ppermute | solution.py:14
  146.0 11.2 %copy-start.59 = (s32[8,128]{1,0:T(8,128)S(1)}, s32[8,128]{1,0:T(8,128)}, u32[]{:S(2)}) copy-start(s32[8,128]{1,0:T(8,128)} %copy-done.58) | copy-start | bytes 12292
  146.0 11.2 %copy-start.95 = (s32[8]{0:T(128)S(1)}, s32[8]{0:T(128)}, u32[]{:S(2)}) copy-start(s32[8]{0:T(128)} %copy-done.94) | copy-start | bytes 100
  147.8 7.4 %copy-start.52 = (bf16[258,512]{1,0:T(8,128)(2,1)}, bf16[258,512]{1,0:T(8,128)(2,1)S(1)}, u32[]{:S(2)}) copy-start(bf16[258,512]{1,0:T(8,128)(2,1)S(1)} %collective-permute-done.3) | copy-start | bytes 792580
  157.2 3.8 %copy-start.53 = (bf16[258,512]{1,0:T(8,128)(2,1)S(1)}, bf16[258,512]{1,0:T(8,128)(2,1)}, u32[]{:S(2)}) copy-start(bf16[258,512]{1,0:T(8,128)(2,1)} %copy-done.52) | copy-start | bytes 792580
  163.2 4.6 %copy-start.4 = (bf16[4,256,512]{1,2,0:T(8,128)(2,1)S(1)}, bf16[4,256,512]{1,2,0:T(8,128)(2,1)}, u32[]{:S(2)}) copy-start(bf16[4,256,512]{1,2,0:T(8,128)(2,1)} %copy-done.2) | copy-start | bytes 3145732
  167.8 51.6 %reduce-scatter.9.cloned.1.call-start = ((), (), s32[]{:S(2)}) async-start(), calls=%async_computation.10 | async-start | bytes 1310720 | tf_op jit(solution)/shard_map/reduce_scatter | solution.py:142
  169.9 2.6 copy-start.29
  178.6 2.6 copy-start.99
  178.7 66.6 %reduce-scatter.7.cloned.1.call-start = ((), (), s32[]{:S(2)}) async-start(), calls=%async_computation.9 | async-start | bytes 1310720 | tf_op jit(solution)/shard_map/reduce_scatter | solution.py:142
  182.7 2.5 copy-start.105
  185.2 4.7 %copy-start.6 = (bf16[2048,256]{1,0:T(8,128)(2,1)S(1)}, bf16[2048,256]{1,0:T(8,128)(2,1)}, u32[]{:S(2)}) copy-start(bf16[2048,256]{1,0:T(8,128)(2,1)} %param.19) | copy-start | bytes 3145732
  189.8 81.1 %reduce-scatter.5.cloned.1.call-start = ((), (), s32[]{:S(2)}) async-start(), calls=%async_computation.8 | async-start | bytes 1310720 | tf_op jit(solution)/shard_map/reduce_scatter | solution.py:142
  189.9 2.8 %copy-start.34 = (f32[1,256,512]{2,1,0:T(8,128)S(1)}, f32[1,256,512]{2,1,0:T(8,128)}, u32[]{:S(2)}) copy-start(f32[1,256,512]{2,1,0:T(8,128)} %get-tuple-element.57) | copy-start | bytes 1572868
  189.9 2.8 %copy-start.35 = (f32[1,256,512]{2,1,0:T(8,128)S(1)}, f32[1,256,512]{2,1,0:T(8,128)}, u32[]{:S(2)}) copy-start(f32[1,256,512]{2,1,0:T(8,128)} %get-tuple-element.58) | copy-start | bytes 1572868
  189.9 2.8 %copy-start.36 = (f32[1,256,512]{2,1,0:T(8,128)S(1)}, f32[1,256,512]{2,1,0:T(8,128)}, u32[]{:S(2)}) copy-start(f32[1,256,512]{2,1,0:T(8,128)} %get-tuple-element.59) | copy-start | bytes 1572868
  189.9 2.8 %copy-start.98 = (f32[4,64]{1,0:T(4,128)S(1)}, f32[4,64]{1,0:T(4,128)}, u32[]{:S(2)}) copy-start(f32[4,64]{1,0:T(4,128)} %get-tuple-element.82) | copy-start | bytes 3076
  (56 other events, 94.8 us)
Sparse Core Ops, SparseCore 0:
  167.9 25.5 reduce-scatter.10
  195.9 23.4 reduce-scatter.8
  221.8 23.4 reduce-scatter.6
  247.5 23.3 reduce-scatter.4
